TPU v7x, 32 devices: a whole 2x2x4 slice. The times are simulated.
32 devices in a mesh: groups: 2 (over y), seq: 4 (over z), chan: 4 (over x, core).
Axes of the slice: x: 2, y: 2, z: 4, core: 2. Of those that a mesh axis runs over, the one named last changes fastest.
Arguments:
- value: bfloat16 [1024, 4096], P(('groups', 'seq'), 'chan'), parts along dimension 0, may hold values from -6 to 6
- first_gate: bfloat16 [1024, 4096], P(('groups', 'seq'), 'chan'), parts along dimension 0, may hold values from -6 to 6
- second_gate: bfloat16 [1024, 4096], P(('groups', 'seq'), 'chan'), parts along dimension 0, may hold values from -6 to 6
- first_filter: bfloat16 [256, 512], P('chan'), may hold values from -0.25 to 0.25
- second_filter: bfloat16 [256, 512], P('chan'), may hold values from -0.25 to 0.25
- out_weight: bfloat16 [4096, 4096], P('chan'), may hold values from -0.09375 to 0.09375
- segment_ids: int32 [1024], P(('groups', 'seq')), parts along dimension 0, may hold values from 0 to 1, never falling along the last dimension, each value on 1 to 384 neighbouring positions
Outputs:
- mixed: bfloat16 [1024, 4096], P(('groups', 'seq')), parts along dimension 0
There are 2 independent parts, one for each index of `groups`. A program takes and returns all parts, laid end to end along the dimension named above; an argument that names none is the same for every part. Nothing has to cross between parts.
Inputs may be any that keep to these rules, and one draw needn't show every extreme that they name: `segment_ids`: ids never fall along the window; the 2 contexts each hold 128 to 384 neighbouring positions and together fill the window.
All inputs are finite; a program needn't handle non-finite values.
Results may differ from a plain program's by a relative error of at most 0.0065.
Values may be sent and summed in bfloat16 or wider, within the bound.
No kernel may reach another device: no remote copies, remote signals or barrier semaphores. Data moves between devices by JAX's collectives and lax.ppermute only.
A program may use at most 192 MiB of HBM per device.

v0:
```python
import numpy as np
import jax
import jax.numpy as jnp
from jax import lax
from jax.sharding import PartitionSpec as P

F32 = jnp.float32
BF16 = jnp.bfloat16


def split_bf16(mat):
    hi = mat.astype(jnp.bfloat16)
    lo = (mat - hi.astype(np.float64)).astype(jnp.bfloat16)
    return (hi, lo)


def dft_mats(length):
    half = length // 2
    n = np.arange(length)
    f = np.arange(half)
    ang = 2.0 * np.pi * (f[:, None] * n[None, :] % length) / length
    fwd = np.zeros((length, length))
    fwd[:half] = np.cos(ang)
    fwd[half] = np.where(n % 2 == 0, 1.0, -1.0)
    fwd[half + 1 :] = -np.sin(ang[1:])
    inv = np.zeros((length, length))
    scale = np.full(half, 2.0)
    scale[0] = 1.0
    inv[:, :half] = (np.cos(ang) * scale[:, None]).T / length
    inv[:, half] = np.where(n % 2 == 0, 1.0, -1.0) / length
    inv[:, half + 1 :] = (-2.0 * np.sin(ang[1:])).T / length
    return (split_bf16(fwd), split_bf16(inv))


def mm(a, b):
    return jnp.dot(a, b, preferred_element_type=F32)


def swap(x, bit):
    return lax.ppermute(x, "chan", [(c, c ^ bit) for c in range(4)])


def make_local(nseq, nchan):

    def local(value, first_gate, second_gate, first_filter, second_filter, out_weight, segment_ids):
        chans = value.shape[1]
        filt_local, length = first_filter.shape
        group = chans // filt_local
        per = chans // nseq
        fpd = per // group
        half = length // 2
        (f_hi, f_lo), (i_hi, i_lo) = dft_mats(length)
        f_hi, f_lo, i_hi, i_lo = (jnp.asarray(m) for m in (f_hi, f_lo, i_hi, i_lo))
        me = lax.axis_index("seq")

        def spectrum(filt):
            mine = lax.dynamic_slice_in_dim(filt, me * fpd, fpd, 0)
            taps = jnp.repeat(mine.T, group, axis=1)
            spec = mm(f_hi, taps) + mm(f_lo, taps)
            re, im = (spec[:half], spec[half:])
            row0 = lax.broadcasted_iota(jnp.int32, re.shape, 0) == 0
            a = re
            b = jnp.where(row0, 0.0, im)
            d = jnp.where(row0, im, re)
            two = lambda x: jnp.concatenate([x, x], axis=1)
            return (two(a), two(b), two(d))

        def long_conv(spec, field):
            a, b, d = spec
            zero = jnp.zeros_like(field)
            masked = jnp.concatenate(
                [jnp.where(in0, field, zero), jnp.where(in1, field, zero)], axis=1
            )
            x = mm(f_hi, masked) + mm(f_lo, masked)
            xr, xi = (x[:half], x[half:])
            y = jnp.concatenate([xr * a - xi * b, xr * b + xi * d], axis=0)
            y_hi32 = lax.reduce_precision(y, exponent_bits=8, mantissa_bits=7)
            y_hi = y_hi32.astype(BF16)
            y_lo = (y - y_hi32).astype(BF16)
            both = mm(i_hi, y_hi) + mm(i_hi, y_lo) + mm(i_lo, y_hi)
            return jnp.where(in0, both[:, :per], 0.0) + jnp.where(in1, both[:, per:], 0.0)

        rows = value.shape[0]
        first_input = (first_gate.astype(F32) * value.astype(F32)).astype(BF16)
        first_input = first_input.reshape(rows, nseq, per).transpose(1, 0, 2)
        id_rows = -(-rows // per)
        pad_rows = -(-id_rows // 16) * 16
        ids = jnp.pad(segment_ids.astype(BF16), (0, pad_rows * per - rows)).reshape(
            1, pad_rows, per
        )
        payload = jnp.concatenate(
            [first_input, jnp.broadcast_to(ids, (nseq, pad_rows, per))], axis=1
        )
        got = lax.all_to_all(payload, "seq", 0, 0, tiled=True)
        first_cols = got[:, :rows].reshape(nseq * rows, per)
        segs = got[:, rows:].reshape(nseq, pad_rows * per)[:, :rows].reshape(nseq * rows)
        in0 = (segs == 0)[:, None]
        in1 = (segs == 1)[:, None]
        gate_blocks = second_gate.reshape(rows, nseq, per).transpose(1, 0, 2)
        gate_cols = lax.all_to_all(gate_blocks, "seq", 0, 0, tiled=True).reshape(nseq * rows, per)
        first_mix = long_conv(spectrum(first_filter), first_cols)
        second_input = (gate_cols.astype(F32) * first_mix).astype(BF16)
        second_mix = long_conv(spectrum(second_filter), second_input).astype(BF16)
        mix_blocks = lax.all_to_all(second_mix.reshape(nseq, rows, per), "seq", 0, 0, tiled=True)
        out_cols = out_weight.shape[1]
        w_blocks = out_weight.reshape(nseq, per, out_cols)

        def project(w):
            return lax.dot_general(
                mix_blocks, w, (((0, 2), (0, 1)), ((), ())), preferred_element_type=F32
            )

        if nchan != 4:
            return lax.psum(project(w_blocks), "chan").astype(BF16)
        core = lax.axis_index("chan") % 2
        width = out_cols // 2
        w_halves = w_blocks.reshape(nseq, per, 2, width)
        other = project(lax.dynamic_index_in_dim(w_halves, 1 - core, 2, keepdims=False))
        got_other = swap(other.astype(BF16), 1)
        mine = project(lax.dynamic_index_in_dim(w_halves, core, 2, keepdims=False))
        chip = mine + got_other.astype(F32)
        total = (chip + swap(chip.astype(BF16), 2).astype(F32)).astype(BF16)
        peer = swap(total, 1)
        return jnp.where(
            core == 0, jnp.concatenate([total, peer], 1), jnp.concatenate([peer, total], 1)
        )

    return local


def solution(mesh):
    in_specs = (
        P(("groups", "seq"), "chan"),
        P(("groups", "seq"), "chan"),
        P(("groups", "seq"), "chan"),
        P("chan", None),
        P("chan", None),
        P("chan", None),
        P(("groups", "seq")),
    )
    out_specs = P(("groups", "seq"), None)
    local = make_local(mesh.shape["seq"], mesh.shape["chan"])
    return jax.shard_map(local, mesh=mesh, in_specs=in_specs, out_specs=out_specs, check_vma=False)
```

profile of v0, /device:TPU:0, one launch (start us, length us, event | category | flops | bytes accessed | tf_op | source)
XLA Modules:
  0.0 107.2 jit_solution(14408337115999331326)
XLA Ops:
  0.0 1.1 %multiply_convert_fusion = bf16[128,1024]{1,0:T(8,128)(2,1)S(1)} fusion(bf16[128,1024]{1,0:T(8,128)(2,1)} %param.11, bf16[128,1024]{1,0:T(8,128)(2,1)} %param.12), kind=kLoop, calls=%fused_computation.59 | loop fusion | flops 524288 | bytes 786432 | tf_op jit(solution)/shard_map/convert_element_type | solution.py:84
  2.6 6.3 %all-to-all-start = ((bf16[4,144,256]{2,1,0:T(8,128)(2,1)}), bf16[4,144,256]{2,1,0:T(8,128)(2,1)S(1)}, u32[]{:S(2)}, u32[]{:S(2)}) async-start(bf16[4,144,256]{2,1,0:T(8,128)(2,1)} %pad_maximum_fusion.10), calls=%async_computation | async-start | bytes 589824 | tf_op jit(solution)/shard_map/all_to_all | solution.py:94
  9.7 1.4 %fusion.44 = f32[256,512]{0,1:T(8,128)S(1)} fusion(bf16[512,256]{0,1:T(8,128)(2,1)S(1)} %bitcast.85, bf16[512,512]{1,0:T(8,128)(2,1)} %constant.51.clone), kind=kOutput, calls=%fused_computation.93 | convolution fusion | flops 134217728 | bytes 1310720 | tf_op jit(solution)/shard_map/dot_general | solution.py:36
  11.1 1.4 %fusion.43 = f32[256,512]{0,1:T(8,128)S(1)} fusion(bf16[512,256]{0,1:T(8,128)(2,1)S(1)} %bitcast.87, bf16[512,512]{1,0:T(8,128)(2,1)} %constant.51.clone), kind=kOutput, calls=%fused_computation.92 | convolution fusion | flops 134217728 | bytes 1310720 | tf_op jit(solution)/shard_map/dot_general | solution.py:36
  12.5 1.4 %fusion.9 = f32[512,256]{1,0:T(8,128)S(1)} fusion(f32[256,512]{0,1:T(8,128)S(1)} %fusion.44, bf16[512,256]{0,1:T(8,128)(2,1)S(1)} %bitcast.86, bf16[512,512]{1,0:T(8,128)(2,1)} %constant.52.clone), kind=kOutput, calls=%fused_computation.22 | convolution fusion | flops 134348800 | bytes 1835008 | tf_op jit(solution)/shard_map/dot_general | solution.py:36
  13.8 1.4 %fusion.10 = f32[512,256]{1,0:T(8,128)S(1)} fusion(f32[256,512]{0,1:T(8,128)S(1)} %fusion.43, bf16[512,256]{0,1:T(8,128)(2,1)S(1)} %bitcast.88, bf16[512,512]{1,0:T(8,128)(2,1)} %constant.52.clone), kind=kOutput, calls=%fused_computation.24 | convolution fusion | flops 134348800 | bytes 1835008 | tf_op jit(solution)/shard_map/dot_general | solution.py:36
  15.3 14.6 %reshape_reshape.3 = bf16[4,256,2,2048]{3,2,1,0:T(2,128)(2,1)} reshape(bf16[1024,4096]{1,0:T(8,128)(2,1)} %param.16) | data formatting | bytes 16777216 | tf_op jit(solution)/shard_map/reshape;reshape | solution.py:117
  29.9 0.8 copy.40
  30.7 1.2 %slice_select_fusion.6 = (f32[256,256]{1,0:T(8,128)}, f32[256,256]{1,0:T(8,128)}, f32[256,256]{1,0:T(8,128)}, f32[256,256]{1,0:T(8,128)}, f32[256,256]{1,0:T(8,128)}, /*index=5*/f32[256,256]{1,0:T(8,128)}) fusion(f32[512,256]{1,0:T(8,128)S(1)} %fusion.10, pred[256]{0:T(512)(128)(4,1)S(1)} %iota_compare_fusion, f32[512,256]{1,0:T(8,128)S(1)} %fusion.9), kind=kLoop, calls=%fused_computation.70 | loop fusion | flops 262144 | bytes 2621696 | tf_op jit(solution)/shard_map/jit(_where)/select_n | solution.py:64
  32.0 5.2 %all-to-all-start.1 = ((bf16[4,128,256]{1,2,0:T(8,128)(2,1)}), bf16[4,128,256]{1,2,0:T(8,128)(2,1)}, u32[]{:S(2)}, u32[]{:S(2)}) async-start(bf16[4,128,256]{1,2,0:T(8,128)(2,1)} %bitcast.90), calls=%async_computation.1 | async-start | bytes 524288 | tf_op jit(solution)/shard_map/all_to_all | solution.py:100
  38.4 1.6 %fusion.20 = (f32[256,512]{1,0:T(8,128)S(1)}, f32[256,512]{1,0:T(8,128)S(1)}) fusion(f32[256,256]{1,0:T(8,128)} %get-tuple-element.18, f32[256,256]{1,0:T(8,128)} %get-tuple-element.14, f32[512,512]{1,0:T(8,128)S(1)} %fusion.8, f32[256,256]{1,0:T(8,128)} %get-tuple-element.13), kind=kLoop, calls=%fused_computation.44 | loop fusion | flops 1179648 | bytes 2883584 | tf_op jit(solution)/shard_map/sub | solution.py:76
  41.6 4.0 %all-to-all-done.1 = bf16[4,128,256]{1,2,0:T(8,128)(2,1)} async-done(((bf16[4,128,256]{1,2,0:T(8,128)(2,1)}), bf16[4,128,256]{1,2,0:T(8,128)(2,1)}, u32[]{:S(2)}, u32[]{:S(2)}) %all-to-all-start.1) | async-done | bytes 262176 | tf_op jit(solution)/shard_map/all_to_all | solution.py:100
  45.6 1.1 %broadcast_select_fusion.2 = (bf16[512,256]{0,1:T(8,128)(2,1)S(1)}, bf16[512,256]{0,1:T(8,128)(2,1)S(1)}) fusion(pred[512]{0:T(512)(128)(4,1)S(1)} %get-tuple-element.22, f32[512,512]{0,1:T(8,128)S(1)} %fusion.7, pred[512]{0:T(512)(128)(4,1)S(1)} %get-tuple-element.21, bf16[4,128,256]{1,2,0:T(8,128)(2,1)} %all-to-all-done.1), kind=kLoop, calls=%fused_computation.66 | loop fusion | flops 917504 | bytes 1836032 | tf_op jit(solution)/shard_map/jit(_where)/select_n | solution.py:72
  47.7 1.4 %fusion.24 = (f32[256,512]{1,0:T(8,128)S(1)}, f32[256,512]{1,0:T(8,128)S(1)}) fusion(f32[256,256]{1,0:T(8,128)S(1)} %copy-done.4, f32[256,256]{1,0:T(8,128)} %get-tuple-element.24, f32[512,512]{1,0:T(8,128)S(1)} %fusion.6, f32[256,256]{1,0:T(8,128)} %get-tuple-element.25), kind=kLoop, calls=%fused_computation.52 | loop fusion | flops 1179648 | bytes 2883584 | tf_op jit(solution)/shard_map/sub | solution.py:76
  50.8 0.8 copy.61
  51.6 3.6 %all-to-all-start.2 = ((bf16[4,128,256]{2,1,0:T(8,128)(2,1)}), bf16[4,128,256]{2,1,0:T(8,128)(2,1)S(1)}, u32[]{:S(2)}, u32[]{:S(2)}) async-start(bf16[4,128,256]{2,1,0:T(8,128)(2,1)} %bitcast.16), calls=%async_computation.2 | async-start | bytes 524288 | tf_op jit(solution)/shard_map/all_to_all | solution.py:104
  55.2 20.5 %constant_dynamic-slice_fusion = (bf16[4,256,1,2048]{3,2,1,0:T(2,128)(2,1)}, bf16[4,256,1,2048]{3,2,1,0:T(2,128)(2,1)}) fusion(bf16[4,256,2,2048]{3,2,1,0:T(2,128)(2,1)} %reshape_reshape.3, s32[]{:T(128)S(6)} %select_n.82, s32[]{:T(128)S(6)} %select_n.81), kind=kLoop, calls=%fused_computation.80 | loop fusion | bytes 16777224 | tf_op jit(solution)/shard_map/jit(dynamic_index_in_dim)/dynamic_slice | solution.py:118
  75.7 6.0 %fusion.4 = bf16[128,2048]{1,0:T(8,128)(2,1)S(1)} fusion(bf16[4,128,256]{2,1,0:T(8,128)(2,1)S(1)} %all-to-all-done.2, bf16[4,256,1,2048]{3,2,1,0:T(2,128)(2,1)} %get-tuple-element.7), kind=kOutput, calls=%fused_computation.6 | convolution fusion | flops 537133056 | bytes 4980736 | tf_op jit(solution)/shard_map/dot_general | solution.py:109
  81.8 1.9 %collective-permute-done = bf16[128,2048]{1,0:T(8,128)(2,1)S(1)} collective-permute-done((bf16[128,2048]{1,0:T(8,128)(2,1)S(1)}, bf16[128,2048]{1,0:T(8,128)(2,1)S(1)}, u32[]{:S(2)}, u32[]{:S(2)}) %collective-permute-start) | collective-permute-done | bytes 524320 | tf_op jit(solution)/shard_map/ppermute | solution.py:40
  83.7 6.1 %fusion.13 = (bf16[128,2048]{1,0:T(8,128)(2,1)S(1)}, f32[128,2048]{1,0:T(8,128)S(1)}) fusion(bf16[128,2048]{1,0:T(8,128)(2,1)S(1)} %collective-permute-done, bf16[4,128,256]{2,1,0:T(8,128)(2,1)S(1)} %all-to-all-done.2, bf16[4,256,1,2048]{3,2,1,0:T(2,128)(2,1)} %get-tuple-element.8), kind=kOutput, calls=%fused_computation.32 | convolution fusion | flops 537657344 | bytes 6553600 | tf_op jit(solution)/shard_map/dot_general | solution.py:109
  89.8 1.5 %collective-permute-start.1 = (bf16[128,2048]{1,0:T(8,128)(2,1)S(1)}, bf16[128,2048]{1,0:T(8,128)(2,1)S(1)}, u32[]{:S(2)}, u32[]{:S(2)}) collective-permute-start(bf16[128,2048]{1,0:T(8,128)(2,1)S(1)} %get-tuple-element.26), channel_id=1, source_target_pairs={{0,2},{1,3},{2,0},{3,1},{4,6},{5,7},{6,4},{7,5},{8,10},{9,11},{10,... | collective-permute-start | bytes 1572872 | tf_op jit(solution)/shard_map/ppermute | solution.py:40
  91.3 12.5 %collective-permute-done.1 = bf16[128,2048]{1,0:T(8,128)(2,1)S(1)} collective-permute-done((bf16[128,2048]{1,0:T(8,128)(2,1)S(1)}, bf16[128,2048]{1,0:T(8,128)(2,1)S(1)}, u32[]{:S(2)}, u32[]{:S(2)}) %collective-permute-start.1) | collective-permute-done | bytes 524320 | tf_op jit(solution)/shard_map/ppermute | solution.py:40
  104.1 1.9 %collective-permute-done.2 = bf16[128,2048]{1,0:T(8,128)(2,1)S(1)} collective-permute-done((bf16[128,2048]{1,0:T(8,128)(2,1)S(1)}, bf16[128,2048]{1,0:T(8,128)(2,1)S(1)}, u32[]{:S(2)}, u32[]{:S(2)}) %collective-permute-start.2) | collective-permute-done | bytes 524320 | tf_op jit(solution)/shard_map/ppermute | solution.py:40
  106.0 1.2 %maximum_select_fusion = bf16[128,4096]{1,0:T(8,128)(2,1)} fusion(bf16[128,2048]{1,0:T(8,128)(2,1)S(1)} %collective-permute-done.2, bf16[128,2048]{1,0:T(8,128)(2,1)S(1)} %add_convert_fusion, pred[]{:T(512)S(6)} %eq.42), kind=kLoop, calls=%fused_computation.29 | loop fusion | flops 4718592 | bytes 2097153 | tf_op jit(solution)/shard_map/jit(_where)/select_n | solution.py:124
  (45 shorter events, 7.8 us)
Async XLA Ops:
  2.6 29.4 %all-to-all-start = ((bf16[4,144,256]{2,1,0:T(8,128)(2,1)}), bf16[4,144,256]{2,1,0:T(8,128)(2,1)S(1)}, u32[]{:S(2)}, u32[]{:S(2)}) async-start(bf16[4,144,256]{2,1,0:T(8,128)(2,1)} %pad_maximum_fusion.10), calls=%async_computation | async-start | bytes 589824 | tf_op jit(solution)/shard_map/all_to_all | solution.py:94
  15.2 14.6 %copy-start.5 = (bf16[128,1024]{1,0:T(8,128)(2,1)S(1)}, bf16[128,1024]{1,0:T(8,128)(2,1)}, u32[]{:S(2)}) copy-start(bf16[128,1024]{1,0:T(8,128)(2,1)} %param.13) | copy-start | bytes 786436
  15.2 22.2 %copy-start.2 = (bf16[512,512]{1,0:T(8,128)(2,1)S(1)}, bf16[512,512]{1,0:T(8,128)(2,1)}, u32[]{:S(2)}) copy-start(bf16[512,512]{1,0:T(8,128)(2,1)} %constant.51.clone) | copy-start | bytes 1572868
  15.3 22.7 %copy-start.1 = (bf16[512,512]{1,0:T(8,128)(2,1)S(1)}, bf16[512,512]{1,0:T(8,128)(2,1)}, u32[]{:S(2)}) copy-start(bf16[512,512]{1,0:T(8,128)(2,1)} %constant.52.clone) | copy-start | bytes 1572868
  29.9 10.2 %copy-start = (bf16[512,512]{1,0:T(8,128)(2,1)S(1)}, bf16[512,512]{1,0:T(8,128)(2,1)}, u32[]{:S(2)}) copy-start(bf16[512,512]{1,0:T(8,128)(2,1)} %constant.53.clone) | copy-start | bytes 1572868
  32.0 9.1 %copy-start.3 = (bf16[512,512]{1,0:T(8,128)(2,1)S(1)}, bf16[512,512]{1,0:T(8,128)(2,1)}, u32[]{:S(2)}) copy-start(bf16[512,512]{1,0:T(8,128)(2,1)} %constant.54.clone) | copy-start | bytes 1572868
  32.0 13.7 %all-to-all-start.1 = ((bf16[4,128,256]{1,2,0:T(8,128)(2,1)}), bf16[4,128,256]{1,2,0:T(8,128)(2,1)}, u32[]{:S(2)}, u32[]{:S(2)}) async-start(bf16[4,128,256]{1,2,0:T(8,128)(2,1)} %bitcast.90), calls=%async_computation.1 | async-start | bytes 524288 | tf_op jit(solution)/shard_map/all_to_all | solution.py:100
  40.1 7.6 %copy-start.4 = (f32[256,256]{1,0:T(8,128)S(1)}, f32[256,256]{1,0:T(8,128)}, u32[]{:S(2)}) copy-start(f32[256,256]{1,0:T(8,128)} %get-tuple-element.23) | copy-start | bytes 786436
  51.6 24.1 %all-to-all-start.2 = ((bf16[4,128,256]{2,1,0:T(8,128)(2,1)}), bf16[4,128,256]{2,1,0:T(8,128)(2,1)S(1)}, u32[]{:S(2)}, u32[]{:S(2)}) async-start(bf16[4,128,256]{2,1,0:T(8,128)(2,1)} %bitcast.16), calls=%async_computation.2 | async-start | bytes 524288 | tf_op jit(solution)/shard_map/all_to_all | solution.py:104
  81.7 2.0 %collective-permute-start = (bf16[128,2048]{1,0:T(8,128)(2,1)S(1)}, bf16[128,2048]{1,0:T(8,128)(2,1)S(1)}, u32[]{:S(2)}, u32[]{:S(2)}) collective-permute-start(bf16[128,2048]{1,0:T(8,128)(2,1)S(1)} %fusion.4), channel_id=1, source_target_pairs={{0,1},{1,0},{2,3},{3,2},{4,5},{5,4},{6,7},{7,6},{8,9},{9,8},{10,11... | collective-permute-start | bytes 1572872 | tf_op jit(solution)/shard_map/ppermute | solution.py:40
  89.8 14.0 %collective-permute-start.1 = (bf16[128,2048]{1,0:T(8,128)(2,1)S(1)}, bf16[128,2048]{1,0:T(8,128)(2,1)S(1)}, u32[]{:S(2)}, u32[]{:S(2)}) collective-permute-start(bf16[128,2048]{1,0:T(8,128)(2,1)S(1)} %get-tuple-element.26), channel_id=1, source_target_pairs={{0,2},{1,3},{2,0},{3,1},{4,6},{5,7},{6,4},{7,5},{8,10},{9,11},{10,... | collective-permute-start | bytes 1572872 | tf_op jit(solution)/shard_map/ppermute | solution.py:40
  104.0 2.0 %collective-permute-start.2 = (bf16[128,2048]{1,0:T(8,128)(2,1)S(1)}, bf16[128,2048]{1,0:T(8,128)(2,1)S(1)}, u32[]{:S(2)}, u32[]{:S(2)}) collective-permute-start(bf16[128,2048]{1,0:T(8,128)(2,1)S(1)} %add_convert_fusion), channel_id=1, source_target_pairs={{0,1},{1,0},{2,3},{3,2},{4,5},{5,4},{6,7},{7,6},{8,9},{9,8},{10,11... | collective-permute-start | bytes 1572872 | tf_op jit(solution)/shard_map/ppermute | solution.py:40
where the time goes:
time: 108 us; the launch traced here: 107 us
  local copies, waits for them, and re-layouts  37.8 us (35%)
  matrix products  22.4 us (21%)
  waiting for transfers between devices  20.3 us (19%)
  starting transfers between devices  16.8 us (16%)
  other arithmetic  9.49 us (9%)
    dynamic_slice x1, local copies, waits for them, and re-layouts, local(): lax.dynamic_index_in_dim(w_halves, 1 - core, 2, keepdims=False)  20.5 us
    ppermute x3, waiting for transfers between devices, swap(): return lax.ppermute(x, 'chan', [(c, c ^ bit) for c in range(4)])  16.3 us
    another operation x1, local copies, waits for them, and re-layouts, local(): w_halves = w_blocks.reshape(nseq, per, 2, width)  14.6 us
    dot_general x2, matrix products, project(): lax.dot_general(mix_blocks, w, (((0, 2), (0, 1)), ((), ())), preferred_el...  12.1 us
    dot_general x14, matrix products, mm(): return jnp.dot(a, b, preferred_element_type=F32)  10.3 us
    all_to_all x1, starting transfers between devices, local(): got = lax.all_to_all(payload, 'seq', 0, 0, tiled=True)  6.35 us
    all_to_all x1, starting transfers between devices, local(): lax.all_to_all(gate_blocks, 'seq', 0, 0, tiled=True)  5.22 us
    all_to_all x1, waiting for transfers between devices, local(): lax.all_to_all(gate_blocks, 'seq', 0, 0, tiled=True)  4.02 us
  transfers between devices with their start and end apart: 6, of which 4 were waited for; matrix products, arithmetic and copies ran while one was open for 45% of the time, Pallas kernels for 0%

commit v1 on v0

--- a/solution.py
+++ b/solution.py
@@ -6,6 +6,29 @@
 
 F32 = jnp.float32
 BF16 = jnp.bfloat16
+
+
+def in_blocks(x, dim, length):
+    shape = x.shape
+    parts = x.reshape(*shape[:dim], length, shape[dim] // length, *shape[dim + 1 :])
+    return jnp.moveaxis(parts, dim, 0)
+
+
+def joined_along(blocks, dim):
+    lengths = list(blocks.shape[1:])
+    lengths[dim] *= blocks.shape[0]
+    return jnp.moveaxis(blocks, 0, dim).reshape(lengths)
+
+
+def exchange_in_pairs(x, axis, split_dim, concat_dim):
+    size, index = (lax.axis_size(axis), lax.axis_index(axis))
+    pieces = in_blocks(x, split_dim, size)
+    done = [pieces[index]]
+    for step in range(1, size):
+        sent = pieces[index ^ step]
+        done.append(lax.ppermute(sent, axis, [(i, i ^ step) for i in range(size)]))
+    pieces = jnp.stack(done)[index ^ jnp.arange(size)]
+    return joined_along(pieces, concat_dim)
 
 
 def split_bf16(mat):
@@ -97,7 +120,7 @@
         in0 = (segs == 0)[:, None]
         in1 = (segs == 1)[:, None]
         gate_blocks = second_gate.reshape(rows, nseq, per).transpose(1, 0, 2)
-        gate_cols = lax.all_to_all(gate_blocks, "seq", 0, 0, tiled=True).reshape(nseq * rows, per)
+        gate_cols = exchange_in_pairs(gate_blocks, "seq", 0, 0).reshape(nseq * rows, per)
         first_mix = long_conv(spectrum(first_filter), first_cols)
         second_input = (gate_cols.astype(F32) * first_mix).astype(BF16)
         second_mix = long_conv(spectrum(second_filter), second_input).astype(BF16)

time: 108 us -> 101 us (0.935)
  matrix products: 22.4 us -> 18.2 us
  waiting for transfers between devices: 20.3 us -> 16.3 us
  local copies, waits for them, and re-layouts: 37.8 us -> 39.3 us
  other arithmetic: 9.49 us -> 8.37 us
    all_to_all x1 -> x0, starting transfers between devices: 5.22 us -> none  [local(): lax.all_to_all(gate_blocks, 'seq', 0, 0, tiled=True)]
    ppermute x0 -> x3, starting transfers between devices: none -> 4.6 us  [exchange_in_pairs(): done.append(lax.ppermute(sent, axis, [(i, i ^ step) for i in range(size)]))]
    dot_general x14, matrix products: 10.3 us -> 6.16 us  [mm(): return jnp.dot(a, b, preferred_element_type=F32)]
    all_to_all x1 -> x0, waiting for transfers between devices: 4.02 us -> none  [local(): lax.all_to_all(gate_blocks, 'seq', 0, 0, tiled=True)]
    all_to_all x1, starting transfers between devices: 3.59 us -> 5.04 us  [local(): lax.all_to_all(second_mix.reshape(nseq, rows, per), 'seq', 0, 0, tiled=True)]
    sub x2, other arithmetic: 3.08 us -> 1.91 us  [long_conv(): y = jnp.concatenate([xr * a - xi * b, xr * b + xi * d], axis=0)]
  transfers between devices with their start and end apart: 6 -> 8, of which waited for: 4 -> 3; matrix products, arithmetic and copies ran while one was open for 45% -> 42% of each run, Pallas kernels for 0% -> 0%
where the time goes in v1:
time: 101 us; the launch traced here: 100 us
  local copies, waits for them, and re-layouts  39.3 us (39%)
  matrix products  18.2 us (18%)
  starting transfers between devices  17.7 us (18%)
  waiting for transfers between devices  16.3 us (16%)
  other arithmetic  8.37 us (8%)
    dynamic_slice x1, local copies, waits for them, and re-layouts, local(): lax.dynamic_index_in_dim(w_halves, 1 - core, 2, keepdims=False)  20.5 us
    ppermute x3, waiting for transfers between devices, swap(): return lax.ppermute(x, 'chan', [(c, c ^ bit) for c in range(4)])  16.3 us
    another operation x1, local copies, waits for them, and re-layouts, local(): w_halves = w_blocks.reshape(nseq, per, 2, width)  14.6 us
    dot_general x2, matrix products, project(): lax.dot_general(mix_blocks, w, (((0, 2), (0, 1)), ((), ())), preferred_el...  12.1 us
    all_to_all x1, starting transfers between devices, local(): got = lax.all_to_all(payload, 'seq', 0, 0, tiled=True)  6.35 us
    dot_general x14, matrix products, mm(): return jnp.dot(a, b, preferred_element_type=F32)  6.16 us
    all_to_all x1, starting transfers between devices, local(): lax.all_to_all(second_mix.reshape(nseq, rows, per), 'seq', 0, 0, tiled=True)  5.04 us
    ppermute x3, starting transfers between devices, exchange_in_pairs(): done.append(lax.ppermute(sent, axis, [(i, i ^ step) for i in range(size)]))  4.6 us
  transfers between devices with their start and end apart: 8, of which 3 were waited for; matrix products, arithmetic and copies ran while one was open for 42% of the time, Pallas kernels for 0%

profile of v1, /device:TPU:0, one launch (start us, length us, event | category | flops | bytes accessed | tf_op | source)
XLA Modules:
  0.0 100.4 jit_solution(7700127556647194926)
XLA Ops:
  0.0 1.1 %multiply_convert_fusion = bf16[128,1024]{1,0:T(8,128)(2,1)S(1)} fusion(bf16[128,1024]{1,0:T(8,128)(2,1)} %param.11, bf16[128,1024]{1,0:T(8,128)(2,1)} %param.12), kind=kLoop, calls=%fused_computation.59 | loop fusion | flops 524288 | bytes 786432 | tf_op jit(solution)/shard_map/convert_element_type | solution.py:107
  1.1 0.7 convert_element_type.56
  1.8 0.7 pad_maximum_fusion.10
  2.6 6.3 %all-to-all-start = ((bf16[4,144,256]{2,1,0:T(8,128)(2,1)}), bf16[4,144,256]{2,1,0:T(8,128)(2,1)S(1)}, u32[]{:S(2)}, u32[]{:S(2)}) async-start(bf16[4,144,256]{2,1,0:T(8,128)(2,1)} %pad_maximum_fusion.10), calls=%async_computation | async-start | bytes 589824 | tf_op jit(solution)/shard_map/all_to_all | solution.py:117
  8.9 1.1 %copy.40 = bf16[128,1024]{0,1:T(8,128)(2,1)S(1)} copy(bf16[128,1024]{1,0:T(8,128)(2,1)} %param.13) | data formatting | bytes 524288 | tf_op args[2]
  10.2 2.1 %collective-permute-start = (bf16[1,128,256]{2,1,0:T(8,128)(2,1)S(1)}, bf16[1,128,256]{2,1,0:T(8,128)(2,1)}, u32[]{:S(2)}, u32[]{:S(2)}) collective-permute-start(bf16[1,128,256]{2,1,0:T(8,128)(2,1)S(1)} %bitcast.98), channel_id=1, source_target_pairs={{0,4},{4,0},{8,12},{12,8},{1,5},{5,1},{9,13},{13,9},{2,6},{6,2},{1... | collective-permute-start | bytes 196616 | tf_op jit(solution)/shard_map/ppermute | solution.py:29
  12.4 2.4 %collective-permute-start.1 = (bf16[1,128,256]{2,1,0:T(8,128)(2,1)S(1)}, bf16[1,128,256]{2,1,0:T(8,128)(2,1)}, u32[]{:S(2)}, u32[]{:S(2)}) collective-permute-start(bf16[1,128,256]{2,1,0:T(8,128)(2,1)S(1)} %bitcast.99), channel_id=1, source_target_pairs={{0,8},{4,12},{8,0},{12,4},{1,9},{5,13},{9,1},{13,5},{2,10},{6,14},... | collective-permute-start | bytes 196616 | tf_op jit(solution)/shard_map/ppermute | solution.py:29
  15.1 14.6 %reshape_reshape.4 = bf16[4,256,2,2048]{3,2,1,0:T(2,128)(2,1)} reshape(bf16[1024,4096]{1,0:T(8,128)(2,1)} %param.16) | data formatting | bytes 16777216 | tf_op jit(solution)/shard_map/reshape;reshape | solution.py:140
  29.7 0.7 dynamic-slice_bitcast_fusion.1
  32.0 1.2 %slice_select_fusion.6 = (f32[256,256]{1,0:T(8,128)}, f32[256,256]{1,0:T(8,128)}, f32[256,256]{1,0:T(8,128)}, f32[256,256]{1,0:T(8,128)S(1)}, f32[256,256]{1,0:T(8,128)}, /*index=5*/f32[256,256]{1,0:T(8,128)}) fusion(f32[512,256]{1,0:T(8,128)S(1)} %fusion.10, pred[256]{0:T(512)(128)(4,1)S(1)} %iota_compare_fusion, f32[512,256]{1,0:T(8,128)S(1)} %fusion.9), kind=kLoop, calls=%fused_computation.72 | loop fusion | flops 262144 | bytes 2621696 | tf_op jit(solution)/shard_map/jit(_where)/select_n | solution.py:87
  33.2 0.9 maximum_bitcast_fusion
  34.1 0.6 gather_fusion
  36.2 1.7 %fusion.21 = (f32[256,512]{1,0:T(8,128)S(1)}, f32[256,512]{1,0:T(8,128)S(1)}) fusion(f32[256,256]{1,0:T(8,128)} %get-tuple-element.18, f32[256,256]{1,0:T(8,128)} %get-tuple-element.14, f32[512,512]{1,0:T(8,128)S(1)} %fusion.8, f32[256,256]{1,0:T(8,128)} %get-tuple-element.13), kind=kLoop, calls=%fused_computation.45 | loop fusion | flops 1179648 | bytes 2883584 | tf_op jit(solution)/shard_map/sub | solution.py:99
  41.4 0.5 convolution_add_fusion.1
  42.5 0.8 copy.69
  43.3 5.0 %all-to-all-start.1 = ((bf16[4,128,256]{2,1,0:T(8,128)(2,1)}), bf16[4,128,256]{2,1,0:T(8,128)(2,1)S(1)}, u32[]{:S(2)}, u32[]{:S(2)}) async-start(bf16[4,128,256]{2,1,0:T(8,128)(2,1)} %bitcast.25), calls=%async_computation.1 | async-start | bytes 524288 | tf_op jit(solution)/shard_map/all_to_all | solution.py:127
  48.4 20.5 %constant_dynamic-slice_fusion = (bf16[4,256,1,2048]{3,2,1,0:T(2,128)(2,1)}, bf16[4,256,1,2048]{3,2,1,0:T(2,128)(2,1)}) fusion(bf16[4,256,2,2048]{3,2,1,0:T(2,128)(2,1)} %reshape_reshape.4, s32[]{:T(128)S(6)} %select_n.109, s32[]{:T(128)S(6)} %select_n.108), kind=kLoop, calls=%fused_computation.82 | loop fusion | bytes 16777224 | tf_op jit(solution)/shard_map/jit(dynamic_index_in_dim)/dynamic_slice | solution.py:141
  68.9 6.0 %fusion.4 = bf16[128,2048]{1,0:T(8,128)(2,1)S(1)} fusion(bf16[4,128,256]{2,1,0:T(8,128)(2,1)S(1)} %all-to-all-done.1, bf16[4,256,1,2048]{3,2,1,0:T(2,128)(2,1)} %get-tuple-element.7), kind=kOutput, calls=%fused_computation.7 | convolution fusion | flops 537133056 | bytes 4980736 | tf_op jit(solution)/shard_map/dot_general | solution.py:132
  75.0 1.9 %collective-permute-done.3 = bf16[128,2048]{1,0:T(8,128)(2,1)S(1)} collective-permute-done((bf16[128,2048]{1,0:T(8,128)(2,1)S(1)}, bf16[128,2048]{1,0:T(8,128)(2,1)S(1)}, u32[]{:S(2)}, u32[]{:S(2)}) %collective-permute-start.3) | collective-permute-done | bytes 524320 | tf_op jit(solution)/shard_map/ppermute | solution.py:63
  76.9 6.1 %fusion.13 = (bf16[128,2048]{1,0:T(8,128)(2,1)S(1)}, f32[128,2048]{1,0:T(8,128)S(1)}) fusion(bf16[128,2048]{1,0:T(8,128)(2,1)S(1)} %collective-permute-done.3, bf16[4,128,256]{2,1,0:T(8,128)(2,1)S(1)} %all-to-all-done.1, bf16[4,256,1,2048]{3,2,1,0:T(2,128)(2,1)} %get-tuple-element.8), kind=kOutput, calls=%fused_computation.33 | convolution fusion | flops 537657344 | bytes 6553600 | tf_op jit(solution)/shard_map/dot_general | solution.py:132
  82.9 1.6 %collective-permute-start.4 = (bf16[128,2048]{1,0:T(8,128)(2,1)S(1)}, bf16[128,2048]{1,0:T(8,128)(2,1)S(1)}, u32[]{:S(2)}, u32[]{:S(2)}) collective-permute-start(bf16[128,2048]{1,0:T(8,128)(2,1)S(1)} %get-tuple-element.30), channel_id=1, source_target_pairs={{0,2},{1,3},{2,0},{3,1},{4,6},{5,7},{6,4},{7,5},{8,10},{9,11},{10,... | collective-permute-start | bytes 1572872 | tf_op jit(solution)/shard_map/ppermute | solution.py:63
  84.5 12.5 %collective-permute-done.4 = bf16[128,2048]{1,0:T(8,128)(2,1)S(1)} collective-permute-done((bf16[128,2048]{1,0:T(8,128)(2,1)S(1)}, bf16[128,2048]{1,0:T(8,128)(2,1)S(1)}, u32[]{:S(2)}, u32[]{:S(2)}) %collective-permute-start.4) | collective-permute-done | bytes 524320 | tf_op jit(solution)/shard_map/ppermute | solution.py:63
  97.3 1.9 %collective-permute-done.5 = bf16[128,2048]{1,0:T(8,128)(2,1)S(1)} collective-permute-done((bf16[128,2048]{1,0:T(8,128)(2,1)S(1)}, bf16[128,2048]{1,0:T(8,128)(2,1)S(1)}, u32[]{:S(2)}, u32[]{:S(2)}) %collective-permute-start.5) | collective-permute-done | bytes 524320 | tf_op jit(solution)/shard_map/ppermute | solution.py:63
  99.2 1.2 %maximum_select_fusion = bf16[128,4096]{1,0:T(8,128)(2,1)} fusion(bf16[128,2048]{1,0:T(8,128)(2,1)S(1)} %collective-permute-done.5, bf16[128,2048]{1,0:T(8,128)(2,1)S(1)} %add_convert_fusion, pred[]{:T(512)S(6)} %eq.42), kind=kLoop, calls=%fused_computation.30 | loop fusion | flops 4718592 | bytes 2097153 | tf_op jit(solution)/shard_map/jit(_where)/select_n | solution.py:147
  (60 shorter events, 7.7 us)
Async XLA Ops:
  2.6 32.4 %all-to-all-start = ((bf16[4,144,256]{2,1,0:T(8,128)(2,1)}), bf16[4,144,256]{2,1,0:T(8,128)(2,1)S(1)}, u32[]{:S(2)}, u32[]{:S(2)}) async-start(bf16[4,144,256]{2,1,0:T(8,128)(2,1)} %pad_maximum_fusion.10), calls=%async_computation | async-start | bytes 589824 | tf_op jit(solution)/shard_map/all_to_all | solution.py:117
  10.2 23.0 %collective-permute-start = (bf16[1,128,256]{2,1,0:T(8,128)(2,1)S(1)}, bf16[1,128,256]{2,1,0:T(8,128)(2,1)}, u32[]{:S(2)}, u32[]{:S(2)}) collective-permute-start(bf16[1,128,256]{2,1,0:T(8,128)(2,1)S(1)} %bitcast.98), channel_id=1, source_target_pairs={{0,4},{4,0},{8,12},{12,8},{1,5},{5,1},{9,13},{13,9},{2,6},{6,2},{1... | collective-permute-start | bytes 196616 | tf_op jit(solution)/shard_map/ppermute | solution.py:29
  12.4 20.8 %collective-permute-start.1 = (bf16[1,128,256]{2,1,0:T(8,128)(2,1)S(1)}, bf16[1,128,256]{2,1,0:T(8,128)(2,1)}, u32[]{:S(2)}, u32[]{:S(2)}) collective-permute-start(bf16[1,128,256]{2,1,0:T(8,128)(2,1)S(1)} %bitcast.99), channel_id=1, source_target_pairs={{0,8},{4,12},{8,0},{12,4},{1,9},{5,13},{9,1},{13,5},{2,10},{6,14},... | collective-permute-start | bytes 196616 | tf_op jit(solution)/shard_map/ppermute | solution.py:29
  14.9 18.2 %collective-permute-start.2 = (bf16[1,128,256]{2,1,0:T(8,128)(2,1)S(1)}, bf16[1,128,256]{2,1,0:T(8,128)(2,1)}, u32[]{:S(2)}, u32[]{:S(2)}) collective-permute-start(bf16[1,128,256]{2,1,0:T(8,128)(2,1)S(1)} %bitcast.100), channel_id=1, source_target_pairs={{0,12},{4,8},{8,4},{12,0},{1,13},{5,9},{9,5},{13,1},{2,14},{6,10},... | collective-permute-start | bytes 196616 | tf_op jit(solution)/shard_map/ppermute | solution.py:29
  15.1 15.4 %copy-start.2 = (bf16[512,512]{1,0:T(8,128)(2,1)S(1)}, bf16[512,512]{1,0:T(8,128)(2,1)}, u32[]{:S(2)}) copy-start(bf16[512,512]{1,0:T(8,128)(2,1)} %constant.56.clone) | copy-start | bytes 1572868
  15.1 16.1 %copy-start.1 = (bf16[512,512]{1,0:T(8,128)(2,1)S(1)}, bf16[512,512]{1,0:T(8,128)(2,1)}, u32[]{:S(2)}) copy-start(bf16[512,512]{1,0:T(8,128)(2,1)} %constant.57.clone) | copy-start | bytes 1572868
  31.5 6.4 %copy-start = (bf16[512,512]{1,0:T(8,128)(2,1)S(1)}, bf16[512,512]{1,0:T(8,128)(2,1)}, u32[]{:S(2)}) copy-start(bf16[512,512]{1,0:T(8,128)(2,1)} %constant.58.clone) | copy-start | bytes 1572868
  35.0 4.0 %copy-start.3 = (bf16[512,512]{1,0:T(8,128)(2,1)S(1)}, bf16[512,512]{1,0:T(8,128)(2,1)}, u32[]{:S(2)}) copy-start(bf16[512,512]{1,0:T(8,128)(2,1)} %constant.59.clone) | copy-start | bytes 1572868
  37.9 2.7 %copy-start.4 = (f32[256,256]{1,0:T(8,128)S(1)}, f32[256,256]{1,0:T(8,128)}, u32[]{:S(2)}) copy-start(f32[256,256]{1,0:T(8,128)} %get-tuple-element.28) | copy-start | bytes 786436
  37.9 2.7 %copy-start.5 = (f32[256,256]{1,0:T(8,128)S(1)}, f32[256,256]{1,0:T(8,128)}, u32[]{:S(2)}) copy-start(f32[256,256]{1,0:T(8,128)} %get-tuple-element.29) | copy-start | bytes 786436
  43.3 25.5 %all-to-all-start.1 = ((bf16[4,128,256]{2,1,0:T(8,128)(2,1)}), bf16[4,128,256]{2,1,0:T(8,128)(2,1)S(1)}, u32[]{:S(2)}, u32[]{:S(2)}) async-start(bf16[4,128,256]{2,1,0:T(8,128)(2,1)} %bitcast.25), calls=%async_computation.1 | async-start | bytes 524288 | tf_op jit(solution)/shard_map/all_to_all | solution.py:127
  74.9 2.0 %collective-permute-start.3 = (bf16[128,2048]{1,0:T(8,128)(2,1)S(1)}, bf16[128,2048]{1,0:T(8,128)(2,1)S(1)}, u32[]{:S(2)}, u32[]{:S(2)}) collective-permute-start(bf16[128,2048]{1,0:T(8,128)(2,1)S(1)} %fusion.4), channel_id=1, source_target_pairs={{0,1},{1,0},{2,3},{3,2},{4,5},{5,4},{6,7},{7,6},{8,9},{9,8},{10,11... | collective-permute-start | bytes 1572872 | tf_op jit(solution)/shard_map/ppermute | solution.py:63
  82.9 14.0 %collective-permute-start.4 = (bf16[128,2048]{1,0:T(8,128)(2,1)S(1)}, bf16[128,2048]{1,0:T(8,128)(2,1)S(1)}, u32[]{:S(2)}, u32[]{:S(2)}) collective-permute-start(bf16[128,2048]{1,0:T(8,128)(2,1)S(1)} %get-tuple-element.30), channel_id=1, source_target_pairs={{0,2},{1,3},{2,0},{3,1},{4,6},{5,7},{6,4},{7,5},{8,10},{9,11},{10,... | collective-permute-start | bytes 1572872 | tf_op jit(solution)/shard_map/ppermute | solution.py:63
  97.2 2.0 %collective-permute-start.5 = (bf16[128,2048]{1,0:T(8,128)(2,1)S(1)}, bf16[128,2048]{1,0:T(8,128)(2,1)S(1)}, u32[]{:S(2)}, u32[]{:S(2)}) collective-permute-start(bf16[128,2048]{1,0:T(8,128)(2,1)S(1)} %add_convert_fusion), channel_id=1, source_target_pairs={{0,1},{1,0},{2,3},{3,2},{4,5},{5,4},{6,7},{7,6},{8,9},{9,8},{10,11... | collective-permute-start | bytes 1572872 | tf_op jit(solution)/shard_map/ppermute | solution.py:63
